TPU v7x, 512 devices: a whole 4x4x16 slice. The times are simulated.
512 devices in a mesh: grp: 4 (over y), walk: 128 (over x, z, core).
Axes of the slice: x: 4, y: 4, z: 16, core: 2. Of those that a mesh axis runs over, the one named last changes fastest.
Arguments:
- log_grads: float32 [1024, 131072], P('walk', 'grp'), may hold values from -60 to 60, as said below
- energies: float32 [1024], P('walk'), may hold values from -6 to 6
Outputs:
- update: float32 [131072], P(('grp', 'walk'))
Inputs may be any that keep to these rules, and one draw needn't show every extreme that they name: `log_grads`: real-valued gradients, every row and column with its own scale.
All inputs are finite; a program needn't handle non-finite values.
Results may differ from a plain program's by a relative error of at most 0.0003.
Values sent between devices are 32-bit elements; how exact they have to be, the bound alone decides.
No kernel may reach another device: no remote copies, remote signals or barrier semaphores. Data moves between devices by JAX's collectives and lax.ppermute only.
A program may use at most 128 MiB of HBM per device.

v0:
```python
import jax
import jax.numpy as jnp
from jax import lax
from jax.sharding import PartitionSpec as P

WALKERS = 1024
damping = 0.0004


def factor_solve(factor, rhs):
    column = rhs[:, None]
    first = lax.linalg.triangular_solve(factor, column, left_side=True, lower=True)
    second = lax.linalg.triangular_solve(
        factor, first, left_side=True, lower=True, transpose_a=True
    )
    return second[:, 0]


def on_device(log_grads, energies):
    all_energy = lax.all_gather(energies, "walk", axis=0, tiled=True)
    regrouped = lax.all_to_all(log_grads, "walk", split_axis=1, concat_axis=0, tiled=True)
    group_params = regrouped.shape[1] * lax.axis_size("walk")
    total_params = group_params * lax.axis_size("grp")
    root_walkers = jnp.sqrt(jnp.float32(WALKERS))
    column_mean = jnp.mean(regrouped, axis=0, keepdims=True)
    centred = (regrouped - column_mean) / root_walkers
    scaled_energy = (all_energy - jnp.mean(all_energy)) / root_walkers
    local_gram = jnp.dot(centred, centred.T, precision=lax.Precision.HIGHEST)
    identity_mat = jnp.eye(WALKERS, dtype=jnp.float32)
    whole_gram = lax.psum(local_gram, ("grp", "walk"))
    factor = jnp.linalg.cholesky(whole_gram + damping * total_params * identity_mat)
    solved = factor_solve(factor, scaled_energy)
    update = jnp.dot(solved, centred, precision=lax.Precision.HIGHEST)
    return -(total_params / root_walkers) * update


def solution(mesh):
    return jax.shard_map(
        on_device,
        mesh=mesh,
        in_specs=(P("walk", "grp"), P("walk")),
        out_specs=P(("grp", "walk")),
        check_vma=False,
    )
```

profile of v0, /device:TPU:2, one launch (start us, length us, event | category | flops | bytes accessed | tf_op | source)
XLA Modules:
  0.0 932.4 jit_solution(15668519067561449194)
XLA Ops:
  6.5 75.6 %all_to_all.13 = f32[8,128,256]{2,0,1:T(8,128)S(1)} all-to-all(f32[8,128,256]{2,0,1:T(8,128)} %bitcast.329), channel_id=1, replica_groups=mesh['grp'=4,'walk'=128] {'walk'}, dimensions={1} | all-to-all | bytes 2097152 | tf_op jit(solution)/shard_map/all_to_all | solution.py:21
  82.3 5.2 fusion.33
  89.8 208.2 %all-reduce.1 = f32[1024]{0:T(1024)S(1)} all-reduce(f32[1024]{0:T(1024)S(1)} %dynamic-update-slice.47), channel_id=1, replica_groups=mesh['grp'=4,'walk'=128] {'walk'}, use_global_device_ids=true, to_apply=%add.1 | all-reduce | flops 1024 | bytes 8192
  299.2 270.7 %all-reduce.4.cloned.1.call-done = f32[1024,1024]{0,1:T(8,128)} async-done(((f32[1024,1024]{0,1:T(8,128)}), f32[1024,1024]{0,1:T(8,128)}) %all-reduce.4.cloned.1.call-update) | async-done | bytes 4194320 | tf_op jit(solution)/shard_map/psum | solution.py:30
  569.9 4.8 select_add_fusion
  574.7 5.8 copy.4
  580.5 4.5 fusion
  586.9 11.7 %cholesky.222 = f32[128,128]{1,0:T(8,128)S(1)} custom-call(f32[128,128]{1,0:T(8,128)S(1)} %cholesky.577), custom_call_target="Cholesky" | custom-call | tf_op jit(solution)/shard_map/jit(cholesky)/cholesky | solution.py:31
  598.8 9.8 %custom-call.64 = f32[1,128,128]{1,2,0:T(8,128)S(1)} custom-call(f32[1,128,128]{2,1,0:T(8,128)S(1)} %get-tuple-element.40), custom_call_target="InvertDiagBlocksLowerTriangular" | custom-call | tf_op jit(solution)/shard_map/jit(cholesky)/cholesky | solution.py:31
  611.9 11.7 %cholesky.243 = f32[128,128]{1,0:T(8,128)S(1)} custom-call(f32[128,128]{1,0:T(8,128)S(1)} %cholesky.581), custom_call_target="Cholesky" | custom-call | tf_op jit(solution)/shard_map/jit(cholesky)/cholesky | solution.py:31
  623.9 2.5 cholesky.254
  626.4 9.8 %custom-call.65 = f32[1,128,128]{1,2,0:T(8,128)S(1)} custom-call(f32[1,128,128]{2,1,0:T(8,128)S(1)} %get-tuple-element.38), custom_call_target="InvertDiagBlocksLowerTriangular" | custom-call | tf_op jit(solution)/shard_map/jit(cholesky)/cholesky | solution.py:31
  639.0 2.7 convolution_subtract_fusion.1
  641.7 11.7 %cholesky.466 = f32[128,128]{1,0:T(8,128)S(1)} custom-call(f32[128,128]{1,0:T(8,128)S(1)} %cholesky.586), custom_call_target="Cholesky" | custom-call | tf_op jit(solution)/shard_map/jit(cholesky)/cholesky | solution.py:31
  654.2 9.8 %custom-call.66 = f32[1,128,128]{1,2,0:T(8,128)S(1)} custom-call(f32[1,128,128]{2,1,0:T(8,128)S(1)} %get-tuple-element.36), custom_call_target="InvertDiagBlocksLowerTriangular" | custom-call | tf_op jit(solution)/shard_map/jit(cholesky)/cholesky | solution.py:31
  665.3 3.3 convolution_subtract_fusion.2
  668.6 11.7 %cholesky.485 = f32[128,128]{1,0:T(8,128)S(1)} custom-call(f32[128,128]{1,0:T(8,128)S(1)} %cholesky.591), custom_call_target="Cholesky" | custom-call | tf_op jit(solution)/shard_map/jit(cholesky)/cholesky | solution.py:31
  681.1 9.8 %custom-call.67 = f32[1,128,128]{1,2,0:T(8,128)S(1)} custom-call(f32[1,128,128]{2,1,0:T(8,128)S(1)} %get-tuple-element.34), custom_call_target="InvertDiagBlocksLowerTriangular" | custom-call | tf_op jit(solution)/shard_map/jit(cholesky)/cholesky | solution.py:31
  692.0 3.1 convolution_subtract_fusion.3
  695.2 12.1 %cholesky.504 = f32[128,128]{1,0:T(8,128)S(1)} custom-call(f32[128,128]{1,0:T(8,128)S(1)} %cholesky.596), custom_call_target="Cholesky" | custom-call | tf_op jit(solution)/shard_map/jit(cholesky)/cholesky | solution.py:31
  708.1 9.8 %custom-call.68 = f32[1,128,128]{1,2,0:T(8,128)S(1)} custom-call(f32[1,128,128]{2,1,0:T(8,128)S(1)} %get-tuple-element.32), custom_call_target="InvertDiagBlocksLowerTriangular" | custom-call | tf_op jit(solution)/shard_map/jit(cholesky)/cholesky | solution.py:31
  719.0 3.1 convolution_subtract_fusion.4
  722.1 11.7 %cholesky.524 = f32[128,128]{1,0:T(8,128)S(1)} custom-call(f32[128,128]{1,0:T(8,128)S(1)} %cholesky.601), custom_call_target="Cholesky" | custom-call | tf_op jit(solution)/shard_map/jit(cholesky)/cholesky | solution.py:31
  734.6 9.8 %custom-call.69 = f32[1,128,128]{1,2,0:T(8,128)S(1)} custom-call(f32[1,128,128]{2,1,0:T(8,128)S(1)} %get-tuple-element.30), custom_call_target="InvertDiagBlocksLowerTriangular" | custom-call | tf_op jit(solution)/shard_map/jit(cholesky)/cholesky | solution.py:31
  745.4 2.8 convolution_subtract_fusion.5
  748.2 11.7 %cholesky.544 = f32[128,128]{1,0:T(8,128)S(1)} custom-call(f32[128,128]{1,0:T(8,128)S(1)} %cholesky.606), custom_call_target="Cholesky" | custom-call | tf_op jit(solution)/shard_map/jit(cholesky)/cholesky | solution.py:31
  760.7 9.8 %custom-call.70 = f32[1,128,128]{1,2,0:T(8,128)S(1)} custom-call(f32[1,128,128]{2,1,0:T(8,128)S(1)} %get-tuple-element.28), custom_call_target="InvertDiagBlocksLowerTriangular" | custom-call | tf_op jit(solution)/shard_map/jit(cholesky)/cholesky | solution.py:31
  773.6 11.7 %cholesky.562 = f32[128,128]{1,0:T(8,128)S(1)} custom-call(f32[128,128]{1,0:T(8,128)S(1)} %convolution_subtract_fusion.6), custom_call_target="Cholesky" | custom-call | tf_op jit(solution)/shard_map/jit(cholesky)/cholesky | solution.py:31
  795.8 4.8 select_select_fusion
  800.6 23.7 %while.1 = (s32[]{:T(128)}, f32[1024,1024]{0,1:T(8,128)}, s32[8,2]{0,1:T(2,128)S(1)}, f32[8,128,128]{2,1,0:T(8,128)S(1)}, s32[]{:T(128)}) while((s32[]{:T(128)}, f32[1024,1024]{0,1:T(8,128)}, s32[8,2]{0,1:T(2,128)S(1)}, f32[8,128,128]{2,1,0:T(8,128)S(1)}, s32[]{:T(128)}) %tuple.49), condition=%wide.while_cond, body=%wide.while_body.sunk | while | flops 2 | bytes 393329 | solution.py:13
  813.1 2.2 dynamic-slice.8
  824.3 78.8 %custom-call.71 = f32[8,128,128]{1,2,0:T(8,128)S(1)} custom-call(f32[8,128,128]{2,1,0:T(8,128)S(1)} %get-tuple-element.12), custom_call_target="InvertDiagBlocksLowerTriangular" | custom-call | tf_op jit(solution)/shard_map/triangular_solve | solution.py:13
  (157 shorter events, 70.8 us)
Async XLA Ops:
  6.5 563.4 %all-reduce.4.cloned.1.call-start = ((), (), s32[]{:S(2)}) async-start(), calls=%async_computation.1 | async-start | bytes 8388608 | tf_op jit(solution)/shard_map/psum | solution.py:30
  82.3 7.2 copy-start.1
  585.0 1.9 copy-start
Sparse Core Ops, SparseCore 0:
  87.7 482.1 all-reduce.3
where the time goes:
time: 938 us; the launch traced here: 932 us
  blocking collectives  284 us (30%)
  waiting for transfers between devices  271 us (29%)
  other arithmetic  262 us (28%)
  matrix products  53.4 us (6%)
  local copies, waits for them, and re-layouts  42 us (4%)
  between operations  20.3 us (2%)
    psum x1, waiting for transfers between devices, on_device(): whole_gram = lax.psum(local_gram, ('grp', 'walk'))  271 us
    unnamed x1, blocking collectives  208 us
    another operation x30, other arithmetic, on_device(): jnp.linalg.cholesky(whole_gram + damping * total_params * identity_mat)  168 us
    another operation x3, other arithmetic, factor_solve(): lax.linalg.triangular_solve(factor, first, left_side=True, lower=True, tr...  83.6 us
    all_to_all x1, blocking collectives, on_device(): lax.all_to_all(log_grads, 'walk', split_axis=1, concat_axis=0, tiled=True)  75.6 us
    another operation x14, matrix products, on_device(): jnp.linalg.cholesky(whole_gram + damping * total_params * identity_mat)  27 us
    another operation x40, local copies, waits for them, and re-layouts  23.5 us
  transfers between devices with their start and end apart: 1, of which 1 were waited for; matrix products, arithmetic and copies ran while one was open for 0% of the time, Pallas kernels for 0%

commit v1 on v0

--- a/solution.py
+++ b/solution.py
@@ -5,6 +5,11 @@
 
 WALKERS = 1024
 damping = 0.0004
+
+
+def by_each_axis(x, one, other):
+    partial = lax.psum(x, one)
+    return lax.psum(partial, other)
 
 
 def factor_solve(factor, rhs):
@@ -27,7 +32,7 @@
     scaled_energy = (all_energy - jnp.mean(all_energy)) / root_walkers
     local_gram = jnp.dot(centred, centred.T, precision=lax.Precision.HIGHEST)
     identity_mat = jnp.eye(WALKERS, dtype=jnp.float32)
-    whole_gram = lax.psum(local_gram, ("grp", "walk"))
+    whole_gram = by_each_axis(local_gram, "walk", "grp")
     factor = jnp.linalg.cholesky(whole_gram + damping * total_params * identity_mat)
     solved = factor_solve(factor, scaled_energy)
     update = jnp.dot(solved, centred, precision=lax.Precision.HIGHEST)

time: 938 us -> 1060 us (1.13)
  the two profiles are of different devices: /device:TPU:2 before, /device:TPU:8 now
where the time goes in v1:
time: 1060 us; the launch traced here: 1050 us
  waiting for transfers between devices  350 us (33%)
  blocking collectives  325 us (31%)
  other arithmetic  262 us (25%)
  matrix products  53.3 us (5%)
  local copies, waits for them, and re-layouts  42 us (4%)
  between operations  20.3 us (2%)
    psum x1, waiting for transfers between devices, by_each_axis(): partial = lax.psum(x, one)  350 us
    unnamed x1, blocking collectives  250 us
    another operation x30, other arithmetic, on_device(): jnp.linalg.cholesky(whole_gram + damping * total_params * identity_mat)  168 us
    another operation x3, other arithmetic, factor_solve(): lax.linalg.triangular_solve(factor, first, left_side=True, lower=True, tr...  83.6 us
    all_to_all x1, blocking collectives, on_device(): lax.all_to_all(log_grads, 'walk', split_axis=1, concat_axis=0, tiled=True)  75.4 us
    another operation x14, matrix products, on_device(): jnp.linalg.cholesky(whole_gram + damping * total_params * identity_mat)  27 us
    another operation x40, local copies, waits for them, and re-layouts  23.5 us
  transfers between devices with their start and end apart: 2, of which 1 were waited for; matrix products, arithmetic and copies ran while one was open for 0% of the time, Pallas kernels for 0%

profile of v1, /device:TPU:8, one launch (start us, length us, event | category | flops | bytes accessed | tf_op | source)
XLA Modules:
  0.0 1053.3 jit_solution(9512195640686240654)
XLA Ops:
  6.5 75.4 %all_to_all.13 = f32[8,128,256]{2,0,1:T(8,128)S(1)} all-to-all(f32[8,128,256]{2,0,1:T(8,128)} %bitcast.329), channel_id=1, replica_groups=mesh['grp'=4,'walk'=128] {'walk'}, dimensions={1} | all-to-all | bytes 2097152 | tf_op jit(solution)/shard_map/all_to_all | solution.py:26
  82.1 5.2 fusion.33
  87.4 350.1 %all-reduce.5.cloned.1.call-done = f32[1024,1024]{0,1:T(8,128)} async-done(((f32[1024,1024]{0,1:T(8,128)}), f32[1024,1024]{0,1:T(8,128)}) %all-reduce.5.cloned.1.call-update) | async-done | bytes 4194320 | tf_op jit(solution)/shard_map/psum | solution.py:11
  439.7 249.9 %all-reduce.1 = f32[1024]{0:T(1024)S(1)} all-reduce(f32[1024]{0:T(1024)S(1)} %dynamic-update-slice.47), channel_id=1, replica_groups=mesh['grp'=4,'walk'=128] {'walk'}, use_global_device_ids=true, to_apply=%add.1 | all-reduce | flops 1024 | bytes 8192
  690.8 4.8 select_add_fusion
  695.7 5.8 copy.4
  701.5 4.5 fusion
  707.9 11.7 %cholesky.222 = f32[128,128]{1,0:T(8,128)S(1)} custom-call(f32[128,128]{1,0:T(8,128)S(1)} %cholesky.577), custom_call_target="Cholesky" | custom-call | tf_op jit(solution)/shard_map/jit(cholesky)/cholesky | solution.py:36
  719.7 9.8 custom-call.64
  732.8 11.7 %cholesky.243 = f32[128,128]{1,0:T(8,128)S(1)} custom-call(f32[128,128]{1,0:T(8,128)S(1)} %cholesky.581), custom_call_target="Cholesky" | custom-call | tf_op jit(solution)/shard_map/jit(cholesky)/cholesky | solution.py:36
  744.9 2.5 cholesky.254
  747.4 9.8 custom-call.65
  759.9 2.7 convolution_subtract_fusion.1
  762.6 11.7 %cholesky.466 = f32[128,128]{1,0:T(8,128)S(1)} custom-call(f32[128,128]{1,0:T(8,128)S(1)} %cholesky.586), custom_call_target="Cholesky" | custom-call | tf_op jit(solution)/shard_map/jit(cholesky)/cholesky | solution.py:36
  775.1 9.8 custom-call.66
  786.2 3.3 convolution_subtract_fusion.2
  789.6 11.7 %cholesky.485 = f32[128,128]{1,0:T(8,128)S(1)} custom-call(f32[128,128]{1,0:T(8,128)S(1)} %cholesky.591), custom_call_target="Cholesky" | custom-call | tf_op jit(solution)/shard_map/jit(cholesky)/cholesky | solution.py:36
  802.1 9.8 custom-call.67
  813.0 3.1 convolution_subtract_fusion.3
  816.2 12.1 %cholesky.504 = f32[128,128]{1,0:T(8,128)S(1)} custom-call(f32[128,128]{1,0:T(8,128)S(1)} %cholesky.596), custom_call_target="Cholesky" | custom-call | tf_op jit(solution)/shard_map/jit(cholesky)/cholesky | solution.py:36
  829.0 9.8 custom-call.68
  840.0 3.1 convolution_subtract_fusion.4
  843.0 11.7 %cholesky.524 = f32[128,128]{1,0:T(8,128)S(1)} custom-call(f32[128,128]{1,0:T(8,128)S(1)} %cholesky.601), custom_call_target="Cholesky" | custom-call | tf_op jit(solution)/shard_map/jit(cholesky)/cholesky | solution.py:36
  855.5 9.8 custom-call.69
  866.3 2.8 convolution_subtract_fusion.5
  869.2 11.7 %cholesky.544 = f32[128,128]{1,0:T(8,128)S(1)} custom-call(f32[128,128]{1,0:T(8,128)S(1)} %cholesky.606), custom_call_target="Cholesky" | custom-call | tf_op jit(solution)/shard_map/jit(cholesky)/cholesky | solution.py:36
  881.7 9.8 custom-call.70
  894.5 11.7 %cholesky.562 = f32[128,128]{1,0:T(8,128)S(1)} custom-call(f32[128,128]{1,0:T(8,128)S(1)} %convolution_subtract_fusion.6), custom_call_target="Cholesky" | custom-call | tf_op jit(solution)/shard_map/jit(cholesky)/cholesky | solution.py:36
  916.7 4.8 select_select_fusion
  921.5 23.7 %while.1 = (s32[]{:T(128)}, f32[1024,1024]{0,1:T(8,128)}, s32[8,2]{0,1:T(2,128)S(1)}, f32[8,128,128]{2,1,0:T(8,128)S(1)}, s32[]{:T(128)}) while((s32[]{:T(128)}, f32[1024,1024]{0,1:T(8,128)}, s32[8,2]{0,1:T(2,128)S(1)}, f32[8,128,128]{2,1,0:T(8,128)S(1)}, s32[]{:T(128)}) %tuple.49), condition=%wide.while_cond, body=%wide.while_body.sunk | while | flops 2 | bytes 393329 | solution.py:18
  937.1 2.2 dynamic-slice.8
  945.3 78.8 %custom-call.71 = f32[8,128,128]{1,2,0:T(8,128)S(1)} custom-call(f32[8,128,128]{2,1,0:T(8,128)S(1)} %get-tuple-element.12), custom_call_target="InvertDiagBlocksLowerTriangular" | custom-call | tf_op jit(solution)/shard_map/triangular_solve | solution.py:18
  (160 shorter events, 70.9 us)
Async XLA Ops:
  6.5 430.9 %all-reduce.5.cloned.1.call-start = ((), (), s32[]{:S(2)}) async-start(), calls=%async_computation.1 | async-start | bytes 8388608 | tf_op jit(solution)/shard_map/psum | solution.py:11
  87.3 352.1 %copy-start.1 = (f32[8]{0:T(128)S(1)}, f32[8]{0:T(128)}, u32[]{:S(2)}) copy-start(f32[8]{0:T(128)} %param.3) | copy-start | bytes 100
  87.4 603.5 %all-reduce.7.cloned.1.call-start = ((), (), s32[]{:S(2)}) async-start(), calls=%async_computation.2 | async-start | bytes 8388608 | tf_op jit(solution)/shard_map/psum | solution.py:12
  705.9 1.9 copy-start
Sparse Core Ops, SparseCore 0:
  87.5 349.9 all-reduce.4
  439.9 105.2 all-reduce.6
